TPU v7x, 32 devices: a whole 2x2x4 slice. The times are simulated.
32 devices in a mesh: dp: 16 (over z, x, core), tm: 2 (over y).
Axes of the slice: x: 2, y: 2, z: 4, core: 2. Of those that a mesh axis runs over, the one named last changes fastest.
Arguments:
- src_mel: bfloat16 [2, 128, 640], P('tm', 'dp'), may hold values from -6 to 6
- owner: int32 [2, 128], P('tm', 'dp'), may hold values from 0 to 15, as said below
- dst_pos: int32 [2, 128], P('tm', 'dp'), may hold values from 0 to 7, as said below
- keep: int32 [2, 128], P('tm', 'dp'), may hold values 0 or 1
- cotangent: bfloat16 [16, 1024, 256], P('dp', 'tm'), may hold values from -0.125 to 0.125
- w_pre: bfloat16 [560, 512], replicated, may hold values from -0.25 to 0.25
- b_pre: float32 [512], replicated, may hold values from -3 to 3
- w_ups: bfloat16 [512, 4096], P('tm'), may hold values from -0.1875 to 0.1875
- upsample_bias: float32 [256], replicated, may hold values from -3 to 3
- w_res: bfloat16 [768, 256], replicated, may hold values from -0.21875 to 0.21875
- b_res: float32 [256], replicated, may hold values from -3 to 3
Outputs:
- section_out: bfloat16 [16, 1024, 256], P('dp', 'tm')
- grad_w_pre: float32 [560, 512], replicated
- grad_b_pre: float32 [512], replicated
- grad_w_res: float32 [768, 256], replicated
- grad_b_res: float32 [256], replicated
Inputs may be any that keep to these rules, and one draw needn't show every extreme that they name: Within one tm column, every dp index sends at most one of its segments to each owner, and every owner receives exactly 8 segments. `dst_pos`: the segments received by one owner in one column have positions 0 to 7, each once.
All inputs are finite; a program needn't handle non-finite values. No bound on the sum of `keep` on one device may be relied on, other than what follows from the above.
Results may differ from a plain program's by a relative error of at most 0.009.
The roundings to bfloat16 on the way count: a program that leaves them out, or rounds other values in their place, can miss the bound.
Values may be sent and summed in bfloat16 or wider, within the bound.
No kernel may reach another device: no remote copies, remote signals or barrier semaphores. Data moves between devices by JAX's collectives and lax.ppermute only.
A program may use at most 64 MiB of HBM per device.

v0:
```python
import jax
import jax.numpy as jnp
from jax import lax
from jax.sharding import PartitionSpec as P

KPRE = 7
UPSAMPLE_FACTOR = 8
DILATION_SIZE = 3


def with_halo(block, sides, width):
    for axis, dim in sides:
        count = lax.axis_size(axis)
        forward = [(i, i + 1) for i in range(count - 1)]
        backward = [(target, source) for source, target in forward]
        low = lax.ppermute(
            lax.slice_in_dim(block, block.shape[dim] - width, None, axis=dim), axis, forward
        )
        high = lax.ppermute(lax.slice_in_dim(block, 0, width, axis=dim), axis, backward)
        block = jnp.concatenate([low, block, high], axis=dim)
    return block


def leaky(value):
    return jnp.where(value > 0, value, 0.1 * value)


def negative_slope(value):
    return jnp.where(value > 0, 1.0, 0.1).astype(jnp.float32)


def contract_rows(left, right):
    return lax.dot_general(
        left, right, (((0,), (0,)), ((), ())), preferred_element_type=jnp.float32
    )


def contract_cols(left, right):
    return lax.dot_general(
        left, right, (((1,), (1,)), ((), ())), preferred_element_type=jnp.float32
    )


def local_pass(
    mel_ext,
    gradient_value,
    first_frame0,
    total,
    w_pre,
    b_pre,
    ups_forward,
    ups_backward,
    upsample_bias,
    w_res,
    b_res,
):
    mel_bins = mel_ext.shape[1]
    kpre = w_pre.shape[0] // mel_bins
    edge = kpre // 2 + 1
    frame_count = mel_ext.shape[0] - 2 * edge
    window_width = upsample_bias.shape[0]
    residual_kernel = w_res.shape[0] // window_width
    patches = jnp.concatenate([mel_ext[i : i + frame_count + 2] for i in range(kpre)], axis=1)
    pre = jnp.dot(patches, w_pre, preferred_element_type=jnp.float32) + b_pre
    frame_idx = first_frame0 - 1 + jnp.arange(frame_count + 2, dtype=jnp.int32)
    inside_f = ((frame_idx >= 0) & (frame_idx < total))[:, None]
    act = jnp.where(inside_f, leaky(pre), 0.0).astype(jnp.bfloat16)
    taps = ups_forward(act).reshape(frame_count + 2, 2 * UPSAMPLE_FACTOR, window_width)
    upper_output = taps[1:, :UPSAMPLE_FACTOR] + taps[:-1, UPSAMPLE_FACTOR:]
    sample_count = UPSAMPLE_FACTOR * frame_count
    start_offset = UPSAMPLE_FACTOR // 2 - DILATION_SIZE
    waveform = (
        upper_output.reshape(UPSAMPLE_FACTOR * (frame_count + 1), window_width)[
            start_offset : start_offset + sample_count + 2 * DILATION_SIZE
        ]
        + upsample_bias
    )
    step_index = (
        UPSAMPLE_FACTOR * first_frame0
        - DILATION_SIZE
        + jnp.arange(sample_count + 2 * DILATION_SIZE, dtype=jnp.int32)
    )
    inside_samples = ((step_index >= 0) & (step_index < UPSAMPLE_FACTOR * total))[:, None]
    hidden_state = jnp.where(inside_samples, leaky(waveform), 0.0).astype(jnp.bfloat16)
    column_block = jnp.concatenate(
        [
            hidden_state[kernel_index * DILATION_SIZE : kernel_index * DILATION_SIZE + sample_count]
            for kernel_index in range(residual_kernel)
        ],
        axis=1,
    )
    convolve_fn = jnp.dot(column_block, w_res, preferred_element_type=jnp.float32) + b_res
    output_rows = (waveform[DILATION_SIZE : DILATION_SIZE + sample_count] + convolve_fn).astype(
        jnp.bfloat16
    )
    g_wres = contract_rows(column_block, gradient_value)
    g_bres = jnp.sum(gradient_value.astype(jnp.float32), axis=0)
    backward_pass = contract_cols(gradient_value, w_res)
    hidden_gradient = jnp.zeros((sample_count + 2 * DILATION_SIZE, window_width), jnp.float32)
    for kernel_index in range(residual_kernel):
        hidden_gradient = hidden_gradient + jnp.pad(
            backward_pass[:, kernel_index * window_width : (kernel_index + 1) * window_width],
            (
                (
                    kernel_index * DILATION_SIZE,
                    (residual_kernel - 1 - kernel_index) * DILATION_SIZE,
                ),
                (0, 0),
            ),
        )
    waveform_gradient = jnp.where(
        inside_samples, hidden_gradient * negative_slope(waveform), 0.0
    ) + jnp.pad(gradient_value.astype(jnp.float32), ((DILATION_SIZE, DILATION_SIZE), (0, 0)))
    waveform_gradient = waveform_gradient.astype(jnp.bfloat16)
    d_upper = jnp.pad(waveform_gradient, ((start_offset, start_offset), (0, 0))).reshape(
        frame_count + 1, UPSAMPLE_FACTOR, window_width
    )
    zero_row = jnp.zeros((1, UPSAMPLE_FACTOR, window_width), jnp.bfloat16)
    d_taps = jnp.concatenate(
        [
            jnp.concatenate([zero_row, d_upper], axis=0),
            jnp.concatenate([d_upper, zero_row], axis=0),
        ],
        axis=1,
    )
    d_act = ups_backward(d_taps.reshape(frame_count + 2, 2 * UPSAMPLE_FACTOR * window_width))
    d_pre = jnp.where(inside_f, d_act * negative_slope(pre), 0.0).astype(jnp.bfloat16)
    g_wpre = contract_rows(patches, d_pre)
    g_bpre = jnp.sum(d_pre.astype(jnp.float32), axis=0)
    return (output_rows, (g_wpre, g_bpre, g_wres, g_bres))


def on_device(
    src_mel, owner, dst_pos, keep, cotangent, w_pre, b_pre, w_ups, upsample_bias, w_res, b_res
):
    owners_count = lax.axis_size("dp")
    seg_rows = src_mel[0]
    seg_count = seg_rows.shape[0]
    mel_bins = w_pre.shape[0] // KPRE
    pick = jnp.arange(owners_count, dtype=jnp.int32)[:, None] == owner[0][None, :]
    seg_width = seg_rows.shape[1]
    header = jnp.stack([dst_pos[0] + 1, keep[0]], axis=1).astype(jnp.bfloat16)
    seg_ext = jnp.concatenate([seg_rows, header], axis=1)
    outgoing = jnp.dot(
        pick.astype(jnp.bfloat16), seg_ext, preferred_element_type=jnp.float32
    ).astype(jnp.bfloat16)
    arrived = lax.all_to_all(outgoing, "dp", split_axis=0, concat_axis=0, tiled=True)
    slot_code = arrived[:, seg_width].astype(jnp.int32)
    keep_code = arrived[:, seg_width + 1].astype(jnp.int32)
    place = (slot_code - 1)[:, None] == jnp.arange(seg_count, dtype=jnp.int32)[None, :]
    mel_segs = contract_rows(place.astype(jnp.bfloat16), arrived[:, :seg_width]).astype(
        jnp.bfloat16
    )
    keep_segs = jnp.sum(jnp.where(place, keep_code[:, None], 0), axis=0)
    mel = mel_segs.reshape(seg_count * (mel_segs.shape[1] // mel_bins), mel_bins)
    frame_count = mel.shape[0]
    mel_ext = with_halo(mel, (("tm", 0),), KPRE // 2 + 1)
    first_frame0 = lax.axis_index("tm") * frame_count
    total = lax.axis_size("tm") * frame_count
    cot = cotangent[0]
    marks = jnp.repeat(keep_segs, cot.shape[0] // seg_count)
    gradient_value = jnp.where(marks[:, None] > 0, cot, jnp.zeros_like(cot))
    whole = lax.all_gather(w_ups, "tm", axis=0, tiled=True)

    def ups_forward(act):
        return jnp.dot(act, whole, preferred_element_type=jnp.float32)

    def ups_backward(d_taps):
        return contract_cols(d_taps, whole)

    output_rows, grads = local_pass(
        mel_ext,
        gradient_value,
        first_frame0,
        total,
        w_pre,
        b_pre,
        ups_forward,
        ups_backward,
        upsample_bias,
        w_res,
        b_res,
    )
    summed = lax.psum(grads, ("dp", "tm"))
    return (output_rows[None], summed[0], summed[1], summed[2], summed[3])


def solution(mesh):
    in_specs = (
        P("tm", "dp", None),
        P("tm", "dp"),
        P("tm", "dp"),
        P("tm", "dp"),
        P("dp", "tm", None),
        P(),
        P(),
        P("tm", None),
        P(),
        P(),
        P(),
    )
    out_specs = (P("dp", "tm", None), P(), P(), P(), P())
    return jax.shard_map(
        on_device, mesh=mesh, in_specs=in_specs, out_specs=out_specs, check_vma=False
    )
```

profile of v0, /device:TPU:0, one launch (start us, length us, event | category | flops | bytes accessed | tf_op | source)
XLA Modules:
  0.0 224.1 jit_solution(13383541488804429791)
XLA Ops:
  7.2 0.0 all-gather.2.cloned.1.call-start
  7.3 0.7 all-gather.2.cloned.1.call-update
  8.0 0.1 copy.26
  8.1 0.1 copy.27
  8.2 0.2 fusion.5
  8.4 0.5 broadcast.94
  8.9 0.7 reduce.4
  9.6 0.7 reshape.74
  10.3 7.4 %all-to-all-start = ((bf16[16,2,321]{2,1,0:T(2,128)(2,1)}), bf16[16,2,321]{2,1,0:T(2,128)(2,1)S(1)}, u32[]{:S(2)}, u32[]{:S(2)}) async-start(bf16[16,2,321]{2,1,0:T(2,128)(2,1)} %reshape.74), calls=%async_computation | async-start | bytes 49152 | tf_op jit(solution)/shard_map/all_to_all | solution.py:147
  17.6 0.0 all-reduce.11.cloned.1.call-start
  17.7 6.5 %all-to-all-done = bf16[16,2,321]{2,1,0:T(2,128)(2,1)S(1)} async-done(((bf16[16,2,321]{2,1,0:T(2,128)(2,1)}), bf16[16,2,321]{2,1,0:T(2,128)(2,1)S(1)}, u32[]{:S(2)}, u32[]{:S(2)}) %all-to-all-start) | async-done | bytes 20576 | tf_op jit(solution)/shard_map/all_to_all | solution.py:147
  24.2 0.1 reshape.75
  24.3 0.2 convert_reduce_fusion.2
  24.5 0.1 convolution_convert_fusion.1
  24.6 0.1 reshape.66
  24.7 1.3 collective-permute-start.1
  26.0 0.1 select_reduce_fusion
  26.2 0.1 broadcast_in_dim.91
  26.2 0.1 gt.27
  26.3 0.1 fusion.42
  26.5 0.4 fusion.43
  26.9 0.1 fusion.44
  27.1 4.5 %collective-permute-start = (bf16[4,80]{1,0:T(4,128)(2,1)S(1)}, bf16[4,80]{1,0:T(4,128)(2,1)S(1)}, u32[]{:S(2)}, u32[]{:S(2)}) collective-permute-start(bf16[4,80]{1,0:T(4,128)(2,1)S(1)} %get-tuple-element.27), channel_id=1, source_target_pairs={{0,1},{2,3},{4,5},{6,7},{8,9},{10,11},{12,13},{14,15},{16,17},{18,... | collective-permute-start | bytes 1928 | tf_op jit(solution)/shard_map/ppermute | solution.py:16
  31.6 1.3 collective-permute-done
  33.0 0.1 concatenate.36
  33.1 0.2 convolution_add_fusion.1
  33.4 35.7 %all-gather.2.cloned.1.call-done = bf16[512,4096]{1,0:T(8,128)(2,1)} async-done(((bf16[256,4096]{1,0:T(8,128)(2,1)}), bf16[512,4096]{1,0:T(8,128)(2,1)}) %all-gather.2.cloned.1.call-update) | async-done | bytes 4194320 | tf_op jit(solution)/shard_map/all_gather | solution.py:163
  69.1 3.1 %fusion.19 = f32[66,4096]{1,0:T(8,128)S(1)} fusion(bf16[512,4096]{1,0:T(8,128)(2,1)} %all-gather.2.cloned.1.call-done, f32[66,512]{1,0:T(8,128)S(1)} %convolution_add_fusion.1, pred[66]{0:T(512)(128)(4,1)S(1)} %compare_and_fusion), kind=kOutput, calls=%fused_computation.37 | convolution fusion | flops 276993024 | bytes 5410882 | tf_op jit(solution)/shard_map/dot_general | solution.py:166
  72.2 0.4 copy.30
  72.6 0.1 slice.116
  72.7 0.1 fusion.15
  72.8 0.5 copy-done.12
  73.3 0.3 fusion.12
  73.6 0.1 fusion.14
  73.8 0.1 fusion.45
  73.9 0.1 pad_bitcast_fusion
  74.1 0.2 copy.31
  74.3 1.7 copy-done.1
  75.9 0.0 copy-done.4
  76.0 1.4 convert_reduce_fusion
  77.4 1.3 fusion.48
  78.7 1.4 fusion.16
  80.2 0.2 convert_reduce_fusion.1
  80.3 39.7 %all-reduce.7 = (f32[512]{0:T(512)}, f32[256]{0:T(256)}) all-reduce(f32[512]{0:T(512)S(1)} %get-tuple-element.28, f32[256]{0:T(256)S(1)} %convert_reduce_fusion.1), channel_id=1, replica_groups=mesh['dp'=16,'tm'=2] {'dp','tm'}, use_global_device_ids=true, to_apply=%region_3.4 | all-reduce | flops 768 | bytes 6144 | tf_op jit(solution)/shard_map/psum | solution.py:184
  120.0 1.1 fusion.2
  121.1 92.8 %all-reduce.11.cloned.1.call-done = (f32[560,512]{1,0:T(8,128)}, f32[768,256]{1,0:T(8,128)}) async-done(((f32[560,512]{1,0:T(8,128)}, f32[768,256]{1,0:T(8,128)}), (f32[560,512]{1,0:T(8,128)}, f32[768,256]{1,0:T(8,128)})) %all-reduce.11.cloned.1.call-update) | async-done | bytes 1933328 | tf_op jit(solution)/shard_map/psum | solution.py:184
  213.9 2.4 %copy.38 = f32[560,512]{1,0:T(8,128)} copy(f32[560,512]{1,0:T(8,128)} %get-tuple-element.31) | data formatting | bytes 2293760
  216.3 0.9 copy.39
  (46 shorter events, 0.3 us)
Async XLA Ops:
  7.2 25.9 %copy-start = (bf16[560,512]{1,0:T(8,128)(2,1)S(1)}, bf16[560,512]{1,0:T(8,128)(2,1)}, u32[]{:S(2)}) copy-start(bf16[560,512]{1,0:T(8,128)(2,1)} %param.16) | copy-start | bytes 1720324
  7.2 0.8 copy-start.15
  7.2 0.9 copy-start.16
  7.2 1.0 copy-start.13
  7.2 1.0 copy-start.10
  7.2 19.1 %copy-start.2 = (bf16[1,512,256]{2,1,0:T(8,128)(2,1)S(1)}, bf16[1,512,256]{2,1,0:T(8,128)(2,1)}, u32[]{:S(2)}) copy-start(bf16[1,512,256]{2,1,0:T(8,128)(2,1)} %param.15) | copy-start | bytes 786436
  7.2 19.3 %copy-start.8 = (bf16[768,256]{1,0:T(8,128)(2,1)S(1)}, bf16[768,256]{1,0:T(8,128)(2,1)}, u32[]{:S(2)}) copy-start(bf16[768,256]{1,0:T(8,128)(2,1)} %param.20) | copy-start | bytes 1179652
  7.2 61.9 %all-gather.2.cloned.1.call-start = ((), (), s32[]{:S(2)}) async-start(), calls=%async_computation.1 | async-start | bytes 6291456 | tf_op jit(solution)/shard_map/all_gather | solution.py:163
  10.3 13.9 %all-to-all-start = ((bf16[16,2,321]{2,1,0:T(2,128)(2,1)}), bf16[16,2,321]{2,1,0:T(2,128)(2,1)S(1)}, u32[]{:S(2)}, u32[]{:S(2)}) async-start(bf16[16,2,321]{2,1,0:T(2,128)(2,1)} %reshape.74), calls=%async_computation | async-start | bytes 49152 | tf_op jit(solution)/shard_map/all_to_all | solution.py:147
  17.6 196.3 %all-reduce.11.cloned.1.call-start = ((), (), s32[]{:S(2)}) async-start(), calls=%async_computation.2 | async-start | bytes 3866624 | tf_op jit(solution)/shard_map/psum | solution.py:184
  24.7 6.9 %collective-permute-start.1 = (bf16[4,80]{1,0:T(4,128)(2,1)S(1)}, bf16[4,80]{1,0:T(4,128)(2,1)S(1)}, u32[]{:S(2)}, u32[]{:S(2)}) collective-permute-start(bf16[4,80]{1,0:T(4,128)(2,1)S(1)} %get-tuple-element.26), channel_id=1, source_target_pairs={{1,0},{3,2},{5,4},{7,6},{9,8},{11,10},{13,12},{15,14},{17,16},{19,... | collective-permute-start | bytes 1928 | tf_op jit(solution)/shard_map/ppermute | solution.py:19
  26.9 6.2 %copy-start.11 = (f32[512]{0:T(512)S(1)}, f32[512]{0:T(512)}, u32[]{:S(2)}) copy-start(f32[512]{0:T(512)} %param.17) | copy-start | bytes 6148
  27.1 5.8 %collective-permute-start = (bf16[4,80]{1,0:T(4,128)(2,1)S(1)}, bf16[4,80]{1,0:T(4,128)(2,1)S(1)}, u32[]{:S(2)}, u32[]{:S(2)}) collective-permute-start(bf16[4,80]{1,0:T(4,128)(2,1)S(1)} %get-tuple-element.27), channel_id=1, source_target_pairs={{0,1},{2,3},{4,5},{6,7},{8,9},{10,11},{12,13},{14,15},{16,17},{18,... | collective-permute-start | bytes 1928 | tf_op jit(solution)/shard_map/ppermute | solution.py:16
  33.1 39.1 %copy-start.5 = (bf16[66,560]{1,0:T(8,128)(2,1)}, bf16[66,560]{1,0:T(8,128)(2,1)S(1)}, u32[]{:S(2)}) copy-start(bf16[66,560]{1,0:T(8,128)(2,1)S(1)} %concatenate.36) | copy-start | bytes 221764
  33.4 38.8 %copy-start.3 = (f32[66,512]{1,0:T(8,128)}, f32[66,512]{1,0:T(8,128)S(1)}, u32[]{:S(2)}) copy-start(f32[66,512]{1,0:T(8,128)S(1)} %convolution_add_fusion.1) | copy-start | bytes 405508
  72.6 0.7 copy-start.12
  73.8 2.2 copy-start.1
  74.0 2.0 copy-start.4
  76.0 1.4 copy-start.6
  80.1 39.9 %copy-start.9 = (bf16[768,256]{1,0:T(8,128)(2,1)S(1)}, bf16[768,256]{1,0:T(8,128)(2,1)}, u32[]{:S(2)}) copy-start(bf16[768,256]{1,0:T(8,128)(2,1)} %param.20) | copy-start | bytes 1179652
  80.1 39.9 %copy-start.14 = (f32[256]{0:T(256)S(1)}, f32[256]{0:T(256)}, u32[]{:S(2)}) copy-start(f32[256]{0:T(256)} %param.21) | copy-start | bytes 3076
  213.9 2.4 %copy-start.7 = (f32[768,256]{1,0:T(8,128)S(1)}, f32[768,256]{1,0:T(8,128)}, u32[]{:S(2)}) copy-start(f32[768,256]{1,0:T(8,128)} %get-tuple-element.33) | copy-start | bytes 2359300
Sparse Core Ops, SparseCore 0:
  9.6 59.4 all-gather.1
  80.3 133.6 all-reduce.10
where the time goes:
time: 224 us
  waiting for transfers between devices  137 us (61%)
  blocking collectives  39.7 us (18%)
  between operations  14.4 us (6%)
  starting transfers between devices  13.3 us (6%)
  matrix products  9.26 us (4%)
  local copies, waits for them, and re-layouts  8.51 us (4%)
    psum x1, waiting for transfers between devices, on_device(): summed = lax.psum(grads, ('dp', 'tm'))  92.8 us
    psum x1, blocking collectives, on_device(): summed = lax.psum(grads, ('dp', 'tm'))  39.7 us
    all_gather x1, waiting for transfers between devices, on_device(): whole = lax.all_gather(w_ups, 'tm', axis=0, tiled=True)  35.7 us
    all_to_all x1, starting transfers between devices, on_device(): lax.all_to_all(outgoing, 'dp', split_axis=0, concat_axis=0, tiled=True)  7.36 us
    unnamed x43, local copies, waits for them, and re-layouts  7 us
    all_to_all x1, waiting for transfers between devices, on_device(): lax.all_to_all(outgoing, 'dp', split_axis=0, concat_axis=0, tiled=True)  6.48 us
    ppermute x1, starting transfers between devices, with_halo(): lax.ppermute(lax.slice_in_dim(block, block.shape[dim] - width, None, axis...  4.54 us
  transfers between devices with their start and end apart: 5, of which 4 were waited for; matrix products, arithmetic and copies ran while one was open for 2% of the time, Pallas kernels for 0%

commit v1 on v0

--- a/solution.py
+++ b/solution.py
@@ -6,6 +6,22 @@
 KPRE = 7
 UPSAMPLE_FACTOR = 8
 DILATION_SIZE = 3
+
+
+def swapped_with_each(x, axis, split, join):
+    ways, here = (lax.axis_size(axis), lax.axis_index(axis))
+    width = x.shape[split] // ways
+    lengths = list(x.shape)
+    lengths[split] = width
+    height = lengths[join]
+    lengths[join] = height * ways
+    full = jnp.zeros(lengths, x.dtype)
+    for mask in range(ways):
+        part = lax.dynamic_slice_in_dim(x, (here ^ mask) * width, width, axis=split)
+        if mask:
+            part = lax.ppermute(part, axis, [(d, d ^ mask) for d in range(ways)])
+        full = lax.dynamic_update_slice_in_dim(full, part, (here ^ mask) * height, axis=join)
+    return full
 
 
 def with_halo(block, sides, width):
@@ -144,7 +160,7 @@
     outgoing = jnp.dot(
         pick.astype(jnp.bfloat16), seg_ext, preferred_element_type=jnp.float32
     ).astype(jnp.bfloat16)
-    arrived = lax.all_to_all(outgoing, "dp", split_axis=0, concat_axis=0, tiled=True)
+    arrived = swapped_with_each(outgoing, "dp", 0, 0)
     slot_code = arrived[:, seg_width].astype(jnp.int32)
     keep_code = arrived[:, seg_width + 1].astype(jnp.int32)
     place = (slot_code - 1)[:, None] == jnp.arange(seg_count, dtype=jnp.int32)[None, :]

time: 224 us -> 224 us (level)
  waiting for transfers between devices: 137 us -> 102 us
  local copies, waits for them, and re-layouts: 8.51 us -> 28.9 us
  starting transfers between devices: 13.3 us -> 28.6 us
    all_gather x1, waiting for transfers between devices: 35.7 us -> 6.93 us  [on_device(): whole = lax.all_gather(w_ups, 'tm', axis=0, tiled=True)]
    ppermute x0 -> x15, starting transfers between devices: none -> 22.6 us  [swapped_with_each(): part = lax.ppermute(part, axis, [(d, d ^ mask) for d in range(ways)])]
    dynamic_update_slice x0 -> x16, local copies, waits for them, and re-layouts: none -> 18.7 us  [swapped_with_each(): lax.dynamic_update_slice_in_dim(full, part, (here ^ mask) * height, axis=...]
    all_to_all x1 -> x0, starting transfers between devices: 7.36 us -> none  [on_device(): lax.all_to_all(outgoing, 'dp', split_axis=0, concat_axis=0, tiled=True)]
    all_to_all x1 -> x0, waiting for transfers between devices: 6.48 us -> none  [on_device(): lax.all_to_all(outgoing, 'dp', split_axis=0, concat_axis=0, tiled=True)]
    ppermute x0 -> x15, local copies, waits for them, and re-layouts: none -> 2.8 us  [swapped_with_each(): part = lax.ppermute(part, axis, [(d, d ^ mask) for d in range(ways)])]
    unnamed x43 -> x40, local copies, waits for them, and re-layouts: 7 us -> 6.14 us
  transfers between devices with their start and end apart: 5 -> 19, of which waited for: 4 -> 3; matrix products, arithmetic and copies ran while one was open for 2% -> 11% of each run, Pallas kernels for 0% -> 0%
where the time goes in v1:
time: 224 us
  waiting for transfers between devices  102 us (46%)
  blocking collectives  39.7 us (18%)
  local copies, waits for them, and re-layouts  28.9 us (13%)
  starting transfers between devices  28.6 us (13%)
  between operations  14.7 us (7%)
  matrix products  9.31 us (4%)
    psum x1, waiting for transfers between devices, on_device(): summed = lax.psum(grads, ('dp', 'tm'))  92.8 us
    psum x1, blocking collectives, on_device(): summed = lax.psum(grads, ('dp', 'tm'))  39.7 us
    ppermute x15, starting transfers between devices, swapped_with_each(): part = lax.ppermute(part, axis, [(d, d ^ mask) for d in range(ways)])  22.6 us
    dynamic_update_slice x16, local copies, waits for them, and re-layouts, swapped_with_each(): lax.dynamic_update_slice_in_dim(full, part, (here ^ mask) * height, axis=...  18.7 us
    all_gather x1, waiting for transfers between devices, on_device(): whole = lax.all_gather(w_ups, 'tm', axis=0, tiled=True)  6.93 us
    unnamed x40, local copies, waits for them, and re-layouts  6.14 us
    ppermute x1, starting transfers between devices, with_halo(): lax.ppermute(lax.slice_in_dim(block, block.shape[dim] - width, None, axis...  4.56 us
  transfers between devices with their start and end apart: 19, of which 3 were waited for; matrix products, arithmetic and copies ran while one was open for 11% of the time, Pallas kernels for 0%

profile of v1, /device:TPU:0, one launch (start us, length us, event | category | flops | bytes accessed | tf_op | source)
XLA Modules:
  0.0 224.0 jit_solution(10406328389508127171)
XLA Ops:
  7.3 0.7 all-gather.2.cloned.1.call-update
  8.3 0.2 convolution_convert_fusion
  8.6 0.5 collective-permute-start
  9.1 2.6 %collective-permute-start.1 = (bf16[1,642]{1,0:T(2,128)(2,1)S(1)}, bf16[1,642]{1,0:T(2,128)(2,1)S(1)}, u32[]{:S(2)}, u32[]{:S(2)}) collective-permute-start(bf16[1,642]{1,0:T(2,128)(2,1)S(1)} %get-tuple-element.30), channel_id=1, source_target_pairs={{0,4},{2,6},{4,0},{6,2},{8,12},{10,14},{12,8},{14,10},{16,20},{18,... | collective-permute-start | bytes 3860 | tf_op jit(solution)/shard_map/ppermute | solution.py:22
  11.7 1.8 collective-permute-start.3
  13.6 2.7 %collective-permute-start.5 = (bf16[1,642]{1,0:T(2,128)(2,1)S(1)}, bf16[1,642]{1,0:T(2,128)(2,1)S(1)}, u32[]{:S(2)}, u32[]{:S(2)}) collective-permute-start(bf16[1,642]{1,0:T(2,128)(2,1)S(1)} %get-tuple-element.26), channel_id=1, source_target_pairs={{0,12},{2,14},{4,8},{6,10},{8,4},{10,6},{12,0},{14,2},{16,28},{18,... | collective-permute-start | bytes 3860 | tf_op jit(solution)/shard_map/ppermute | solution.py:22
  16.4 2.6 %collective-permute-start.7 = (bf16[1,642]{1,0:T(2,128)(2,1)S(1)}, bf16[1,642]{1,0:T(2,128)(2,1)S(1)}, u32[]{:S(2)}, u32[]{:S(2)}) collective-permute-start(bf16[1,642]{1,0:T(2,128)(2,1)S(1)} %get-tuple-element.24), channel_id=1, source_target_pairs={{0,16},{2,18},{4,20},{6,22},{8,24},{10,26},{12,28},{14,30},{16,0},... | collective-permute-start | bytes 3860 | tf_op jit(solution)/shard_map/ppermute | solution.py:22
  19.1 3.5 %collective-permute-start.9 = (bf16[1,642]{1,0:T(2,128)(2,1)S(1)}, bf16[1,642]{1,0:T(2,128)(2,1)S(1)}, u32[]{:S(2)}, u32[]{:S(2)}) collective-permute-start(bf16[1,642]{1,0:T(2,128)(2,1)S(1)} %get-tuple-element.22), channel_id=1, source_target_pairs={{0,20},{2,22},{4,16},{6,18},{8,28},{10,30},{12,24},{14,26},{16,4},... | collective-permute-start | bytes 3860 | tf_op jit(solution)/shard_map/ppermute | solution.py:22
  22.8 0.8 dynamic_update_slice.48
  23.7 1.2 dynamic_update_slice.49
  24.9 0.2 copy.38
  25.1 1.2 dynamic_update_slice.50
  26.5 1.2 dynamic_update_slice.51
  27.7 0.5 collective-permute-start.10
  28.2 3.6 %collective-permute-start.11 = (bf16[1,642]{1,0:T(2,128)(2,1)S(1)}, bf16[1,642]{1,0:T(2,128)(2,1)S(1)}, u32[]{:S(2)}, u32[]{:S(2)}) collective-permute-start(bf16[1,642]{1,0:T(2,128)(2,1)S(1)} %get-tuple-element.20), channel_id=1, source_target_pairs={{0,24},{2,26},{4,28},{6,30},{8,16},{10,18},{12,20},{14,22},{16,8},... | collective-permute-start | bytes 3860 | tf_op jit(solution)/shard_map/ppermute | solution.py:22
  31.9 4.4 %collective-permute-start.13 = (bf16[1,642]{1,0:T(2,128)(2,1)S(1)}, bf16[1,642]{1,0:T(2,128)(2,1)S(1)}, u32[]{:S(2)}, u32[]{:S(2)}) collective-permute-start(bf16[1,642]{1,0:T(2,128)(2,1)S(1)} %get-tuple-element.18), channel_id=1, source_target_pairs={{0,28},{2,30},{4,24},{6,26},{8,20},{10,22},{12,16},{14,18},{16,12}... | collective-permute-start | bytes 3860 | tf_op jit(solution)/shard_map/ppermute | solution.py:22
  36.6 1.2 dynamic_update_slice.52
  38.0 1.2 dynamic_update_slice.53
  39.4 1.2 dynamic_update_slice.54
  40.7 1.2 dynamic_update_slice.55
  42.1 1.2 dynamic_update_slice.56
  43.5 1.2 dynamic_update_slice.57
  44.9 1.2 dynamic_update_slice.58
  46.3 1.2 dynamic_update_slice.59
  47.7 1.2 dynamic_update_slice.60
  49.1 1.4 dynamic_update_slice.61
  50.6 1.2 dynamic_update_slice.62
  52.0 1.2 dynamic_update_slice.63
  53.5 1.3 collective-permute-start.16
  55.3 0.4 fusion.45
  55.8 4.6 %collective-permute-start.15 = (bf16[4,80]{1,0:T(4,128)(2,1)S(1)}, bf16[4,80]{1,0:T(4,128)(2,1)S(1)}, u32[]{:S(2)}, u32[]{:S(2)}) collective-permute-start(bf16[4,80]{1,0:T(4,128)(2,1)S(1)} %get-tuple-element.41), channel_id=1, source_target_pairs={{0,1},{2,3},{4,5},{6,7},{8,9},{10,11},{12,13},{14,15},{16,17},{18,... | collective-permute-start | bytes 1928 | tf_op jit(solution)/shard_map/ppermute | solution.py:32
  60.4 1.3 collective-permute-done.15
  61.9 0.2 convolution_add_fusion.1
  62.2 6.9 %all-gather.2.cloned.1.call-done = bf16[512,4096]{1,0:T(8,128)(2,1)} async-done(((bf16[256,4096]{1,0:T(8,128)(2,1)}), bf16[512,4096]{1,0:T(8,128)(2,1)}) %all-gather.2.cloned.1.call-update) | async-done | bytes 4194320 | tf_op jit(solution)/shard_map/all_gather | solution.py:179
  69.1 3.1 %fusion.19 = f32[66,4096]{1,0:T(8,128)S(1)} fusion(bf16[512,4096]{1,0:T(8,128)(2,1)} %all-gather.2.cloned.1.call-done, f32[66,512]{1,0:T(8,128)S(1)} %convolution_add_fusion.1, pred[66]{0:T(512)(128)(4,1)S(1)} %compare_and_fusion), kind=kOutput, calls=%fused_computation.37 | convolution fusion | flops 276993024 | bytes 5410882 | tf_op jit(solution)/shard_map/dot_general | solution.py:182
  72.2 0.4 copy.52
  72.7 0.5 copy-done.12
  73.3 0.3 fusion.11
  73.8 0.2 copy.53
  74.3 1.6 copy-done.1
  75.9 1.4 convert_reduce_fusion
  77.3 1.3 fusion.50
  78.7 1.4 fusion.15
  80.2 39.7 %all-reduce.7 = (f32[512]{0:T(512)}, f32[256]{0:T(256)}) all-reduce(f32[512]{0:T(512)S(1)} %get-tuple-element.42, f32[256]{0:T(256)S(1)} %convert_reduce_fusion.1), channel_id=1, replica_groups=mesh['dp'=16,'tm'=2] {'dp','tm'}, use_global_device_ids=true, to_apply=%region_3.4 | all-reduce | flops 768 | bytes 6144 | tf_op jit(solution)/shard_map/psum | solution.py:200
  120.0 1.1 fusion.2
  121.0 92.8 %all-reduce.11.cloned.1.call-done = (f32[560,512]{1,0:T(8,128)}, f32[768,256]{1,0:T(8,128)}) async-done(((f32[560,512]{1,0:T(8,128)}, f32[768,256]{1,0:T(8,128)}), (f32[560,512]{1,0:T(8,128)}, f32[768,256]{1,0:T(8,128)})) %all-reduce.11.cloned.1.call-update) | async-done | bytes 1933328 | tf_op jit(solution)/shard_map/psum | solution.py:200
  213.9 2.4 %copy.73 = f32[560,512]{1,0:T(8,128)} copy(f32[560,512]{1,0:T(8,128)} %get-tuple-element.45) | data formatting | bytes 2293760
  216.3 0.9 copy.74
  (104 shorter events, 5.4 us)
Async XLA Ops:
  7.2 54.7 %copy-start = (bf16[560,512]{1,0:T(8,128)(2,1)S(1)}, bf16[560,512]{1,0:T(8,128)(2,1)}, u32[]{:S(2)}) copy-start(bf16[560,512]{1,0:T(8,128)(2,1)} %param.16) | copy-start | bytes 1720324
  7.2 0.9 copy-start.15
  7.2 1.0 copy-start.16
  7.2 1.1 copy-start.13
  7.2 1.1 copy-start.10
  7.2 61.9 %all-gather.2.cloned.1.call-start = ((), (), s32[]{:S(2)}) async-start(), calls=%async_computation | async-start | bytes 6291456 | tf_op jit(solution)/shard_map/all_gather | solution.py:179
  8.0 205.9 %all-reduce.11.cloned.1.call-start = ((), (), s32[]{:S(2)}) async-start(), calls=%async_computation.1 | async-start | bytes 3866624 | tf_op jit(solution)/shard_map/psum | solution.py:200
  8.6 5.0 %collective-permute-start = (bf16[1,642]{1,0:T(2,128)(2,1)S(1)}, bf16[1,642]{1,0:T(2,128)(2,1)S(1)}, u32[]{:S(2)}, u32[]{:S(2)}) collective-permute-start(bf16[1,642]{1,0:T(2,128)(2,1)S(1)} %get-tuple-element.31), channel_id=1, source_target_pairs={{0,2},{2,0},{4,6},{6,4},{8,10},{10,8},{12,14},{14,12},{16,18},{18,... | collective-permute-start | bytes 3860 | tf_op jit(solution)/shard_map/ppermute | solution.py:22
  9.1 7.2 %collective-permute-start.1 = (bf16[1,642]{1,0:T(2,128)(2,1)S(1)}, bf16[1,642]{1,0:T(2,128)(2,1)S(1)}, u32[]{:S(2)}, u32[]{:S(2)}) collective-permute-start(bf16[1,642]{1,0:T(2,128)(2,1)S(1)} %get-tuple-element.30), channel_id=1, source_target_pairs={{0,4},{2,6},{4,0},{6,2},{8,12},{10,14},{12,8},{14,10},{16,20},{18,... | collective-permute-start | bytes 3860 | tf_op jit(solution)/shard_map/ppermute | solution.py:22
  11.7 4.7 %collective-permute-start.2 = (bf16[1,642]{1,0:T(2,128)(2,1)S(1)}, bf16[1,642]{1,0:T(2,128)(2,1)S(1)}, u32[]{:S(2)}, u32[]{:S(2)}) collective-permute-start(bf16[1,642]{1,0:T(2,128)(2,1)S(1)} %get-tuple-element.29), channel_id=1, source_target_pairs={{0,6},{2,4},{4,2},{6,0},{8,14},{10,12},{12,10},{14,8},{16,22},{18,... | collective-permute-start | bytes 3860 | tf_op jit(solution)/shard_map/ppermute | solution.py:22
  11.7 7.3 %collective-permute-start.3 = (bf16[1,642]{1,0:T(2,128)(2,1)S(1)}, bf16[1,642]{1,0:T(2,128)(2,1)S(1)}, u32[]{:S(2)}, u32[]{:S(2)}) collective-permute-start(bf16[1,642]{1,0:T(2,128)(2,1)S(1)} %get-tuple-element.28), channel_id=1, source_target_pairs={{0,8},{2,10},{4,12},{6,14},{8,0},{10,2},{12,4},{14,6},{16,24},{18,... | collective-permute-start | bytes 3860 | tf_op jit(solution)/shard_map/ppermute | solution.py:22
  13.6 5.5 %collective-permute-start.4 = (bf16[1,642]{1,0:T(2,128)(2,1)S(1)}, bf16[1,642]{1,0:T(2,128)(2,1)S(1)}, u32[]{:S(2)}, u32[]{:S(2)}) collective-permute-start(bf16[1,642]{1,0:T(2,128)(2,1)S(1)} %get-tuple-element.27), channel_id=1, source_target_pairs={{0,10},{2,8},{4,14},{6,12},{8,2},{10,0},{12,6},{14,4},{16,26},{18,... | collective-permute-start | bytes 3860 | tf_op jit(solution)/shard_map/ppermute | solution.py:22
  13.6 14.1 %collective-permute-start.5 = (bf16[1,642]{1,0:T(2,128)(2,1)S(1)}, bf16[1,642]{1,0:T(2,128)(2,1)S(1)}, u32[]{:S(2)}, u32[]{:S(2)}) collective-permute-start(bf16[1,642]{1,0:T(2,128)(2,1)S(1)} %get-tuple-element.26), channel_id=1, source_target_pairs={{0,12},{2,14},{4,8},{6,10},{8,4},{10,6},{12,0},{14,2},{16,28},{18,... | collective-permute-start | bytes 3860 | tf_op jit(solution)/shard_map/ppermute | solution.py:22
  16.2 12.0 %collective-permute-start.6 = (bf16[1,642]{1,0:T(2,128)(2,1)S(1)}, bf16[1,642]{1,0:T(2,128)(2,1)S(1)}, u32[]{:S(2)}, u32[]{:S(2)}) collective-permute-start(bf16[1,642]{1,0:T(2,128)(2,1)S(1)} %get-tuple-element.25), channel_id=1, source_target_pairs={{0,14},{2,12},{4,10},{6,8},{8,6},{10,4},{12,2},{14,0},{16,30},{18,... | collective-permute-start | bytes 3860 | tf_op jit(solution)/shard_map/ppermute | solution.py:22
  16.4 15.5 %collective-permute-start.7 = (bf16[1,642]{1,0:T(2,128)(2,1)S(1)}, bf16[1,642]{1,0:T(2,128)(2,1)S(1)}, u32[]{:S(2)}, u32[]{:S(2)}) collective-permute-start(bf16[1,642]{1,0:T(2,128)(2,1)S(1)} %get-tuple-element.24), channel_id=1, source_target_pairs={{0,16},{2,18},{4,20},{6,22},{8,24},{10,26},{12,28},{14,30},{16,0},... | collective-permute-start | bytes 3860 | tf_op jit(solution)/shard_map/ppermute | solution.py:22
  19.0 12.9 %collective-permute-start.8 = (bf16[1,642]{1,0:T(2,128)(2,1)S(1)}, bf16[1,642]{1,0:T(2,128)(2,1)S(1)}, u32[]{:S(2)}, u32[]{:S(2)}) collective-permute-start(bf16[1,642]{1,0:T(2,128)(2,1)S(1)} %get-tuple-element.23), channel_id=1, source_target_pairs={{0,18},{2,16},{4,22},{6,20},{8,26},{10,24},{12,30},{14,28},{16,2},... | collective-permute-start | bytes 3860 | tf_op jit(solution)/shard_map/ppermute | solution.py:22
  19.1 17.2 %collective-permute-start.9 = (bf16[1,642]{1,0:T(2,128)(2,1)S(1)}, bf16[1,642]{1,0:T(2,128)(2,1)S(1)}, u32[]{:S(2)}, u32[]{:S(2)}) collective-permute-start(bf16[1,642]{1,0:T(2,128)(2,1)S(1)} %get-tuple-element.22), channel_id=1, source_target_pairs={{0,20},{2,22},{4,16},{6,18},{8,28},{10,30},{12,24},{14,26},{16,4},... | collective-permute-start | bytes 3860 | tf_op jit(solution)/shard_map/ppermute | solution.py:22
  27.7 18.4 %collective-permute-start.10 = (bf16[1,642]{1,0:T(2,128)(2,1)S(1)}, bf16[1,642]{1,0:T(2,128)(2,1)S(1)}, u32[]{:S(2)}, u32[]{:S(2)}) collective-permute-start(bf16[1,642]{1,0:T(2,128)(2,1)S(1)} %get-tuple-element.21), channel_id=1, source_target_pairs={{0,22},{2,20},{4,18},{6,16},{8,30},{10,28},{12,26},{14,24},{16,6},... | collective-permute-start | bytes 3860 | tf_op jit(solution)/shard_map/ppermute | solution.py:22
  28.2 19.2 %collective-permute-start.11 = (bf16[1,642]{1,0:T(2,128)(2,1)S(1)}, bf16[1,642]{1,0:T(2,128)(2,1)S(1)}, u32[]{:S(2)}, u32[]{:S(2)}) collective-permute-start(bf16[1,642]{1,0:T(2,128)(2,1)S(1)} %get-tuple-element.20), channel_id=1, source_target_pairs={{0,24},{2,26},{4,28},{6,30},{8,16},{10,18},{12,20},{14,22},{16,8},... | collective-permute-start | bytes 3860 | tf_op jit(solution)/shard_map/ppermute | solution.py:22
  31.9 17.0 %collective-permute-start.12 = (bf16[1,642]{1,0:T(2,128)(2,1)S(1)}, bf16[1,642]{1,0:T(2,128)(2,1)S(1)}, u32[]{:S(2)}, u32[]{:S(2)}) collective-permute-start(bf16[1,642]{1,0:T(2,128)(2,1)S(1)} %get-tuple-element.19), channel_id=1, source_target_pairs={{0,26},{2,24},{4,30},{6,28},{8,18},{10,16},{12,22},{14,20},{16,10}... | collective-permute-start | bytes 3860 | tf_op jit(solution)/shard_map/ppermute | solution.py:22
  31.9 18.5 %collective-permute-start.13 = (bf16[1,642]{1,0:T(2,128)(2,1)S(1)}, bf16[1,642]{1,0:T(2,128)(2,1)S(1)}, u32[]{:S(2)}, u32[]{:S(2)}) collective-permute-start(bf16[1,642]{1,0:T(2,128)(2,1)S(1)} %get-tuple-element.18), channel_id=1, source_target_pairs={{0,28},{2,30},{4,24},{6,26},{8,20},{10,22},{12,16},{14,18},{16,12}... | collective-permute-start | bytes 3860 | tf_op jit(solution)/shard_map/ppermute | solution.py:22
  36.3 15.5 %collective-permute-start.14 = (bf16[1,642]{1,0:T(2,128)(2,1)S(1)}, bf16[1,642]{1,0:T(2,128)(2,1)S(1)}, u32[]{:S(2)}, u32[]{:S(2)}) collective-permute-start(bf16[1,642]{1,0:T(2,128)(2,1)S(1)} %get-tuple-element.17), channel_id=1, source_target_pairs={{0,30},{2,28},{4,26},{6,24},{8,22},{10,20},{12,18},{14,16},{16,14}... | collective-permute-start | bytes 3860 | tf_op jit(solution)/shard_map/ppermute | solution.py:22
  44.7 10.4 %copy-start.2 = (bf16[1,512,256]{2,1,0:T(8,128)(2,1)S(1)}, bf16[1,512,256]{2,1,0:T(8,128)(2,1)}, u32[]{:S(2)}) copy-start(bf16[1,512,256]{2,1,0:T(8,128)(2,1)} %param.15) | copy-start | bytes 786436
  47.5 7.8 %copy-start.8 = (bf16[768,256]{1,0:T(8,128)(2,1)S(1)}, bf16[768,256]{1,0:T(8,128)(2,1)}, u32[]{:S(2)}) copy-start(bf16[768,256]{1,0:T(8,128)(2,1)} %param.20) | copy-start | bytes 1179652
  53.5 6.9 %collective-permute-start.16 = (bf16[4,80]{1,0:T(4,128)(2,1)S(1)}, bf16[4,80]{1,0:T(4,128)(2,1)S(1)}, u32[]{:S(2)}, u32[]{:S(2)}) collective-permute-start(bf16[4,80]{1,0:T(4,128)(2,1)S(1)} %get-tuple-element.40), channel_id=1, source_target_pairs={{1,0},{3,2},{5,4},{7,6},{9,8},{11,10},{13,12},{15,14},{17,16},{19,... | collective-permute-start | bytes 1928 | tf_op jit(solution)/shard_map/ppermute | solution.py:35
  55.7 6.2 %copy-start.11 = (f32[512]{0:T(512)S(1)}, f32[512]{0:T(512)}, u32[]{:S(2)}) copy-start(f32[512]{0:T(512)} %param.17) | copy-start | bytes 6148
  55.8 5.8 %collective-permute-start.15 = (bf16[4,80]{1,0:T(4,128)(2,1)S(1)}, bf16[4,80]{1,0:T(4,128)(2,1)S(1)}, u32[]{:S(2)}, u32[]{:S(2)}) collective-permute-start(bf16[4,80]{1,0:T(4,128)(2,1)S(1)} %get-tuple-element.41), channel_id=1, source_target_pairs={{0,1},{2,3},{4,5},{6,7},{8,9},{10,11},{12,13},{14,15},{16,17},{18,... | collective-permute-start | bytes 1928 | tf_op jit(solution)/shard_map/ppermute | solution.py:32
  61.9 10.3 %copy-start.5 = (bf16[66,560]{1,0:T(8,128)(2,1)}, bf16[66,560]{1,0:T(8,128)(2,1)S(1)}, u32[]{:S(2)}) copy-start(bf16[66,560]{1,0:T(8,128)(2,1)S(1)} %concatenate.36) | copy-start | bytes 221764
  62.2 10.0 %copy-start.3 = (f32[66,512]{1,0:T(8,128)}, f32[66,512]{1,0:T(8,128)S(1)}, u32[]{:S(2)}) copy-start(f32[66,512]{1,0:T(8,128)S(1)} %convolution_add_fusion.1) | copy-start | bytes 405508
  72.6 0.7 copy-start.12
  73.7 2.2 copy-start.1
  73.8 2.1 copy-start.4
  75.9 1.4 copy-start.6
  80.1 39.9 %copy-start.9 = (bf16[768,256]{1,0:T(8,128)(2,1)S(1)}, bf16[768,256]{1,0:T(8,128)(2,1)}, u32[]{:S(2)}) copy-start(bf16[768,256]{1,0:T(8,128)(2,1)} %param.20) | copy-start | bytes 1179652
  80.1 39.9 %copy-start.14 = (f32[256]{0:T(256)S(1)}, f32[256]{0:T(256)}, u32[]{:S(2)}) copy-start(f32[256]{0:T(256)} %param.21) | copy-start | bytes 3076
  213.9 2.4 %copy-start.7 = (f32[768,256]{1,0:T(8,128)S(1)}, f32[768,256]{1,0:T(8,128)}, u32[]{:S(2)}) copy-start(f32[768,256]{1,0:T(8,128)} %get-tuple-element.47) | copy-start | bytes 2359300
Sparse Core Ops, SparseCore 0:
  9.6 59.4 all-gather.1
  80.2 133.6 all-reduce.10
